TPU v7x, 256 devices: a whole 4x4x8 slice. The times are simulated.
256 devices in a mesh: gx: 64 (over z, x, core), gy: 4 (over y).
Axes of the slice: x: 4, y: 4, z: 8, core: 2. Of those that a mesh axis runs over, the one named last changes fastest.
Arguments:
- volume: bfloat16 [128, 16, 128, 256], P('gx', 'gy'), may hold values from -40 to 40
- void_mask: int32 [128, 16, 128], P('gx', 'gy'), may hold values from 0 to 1, as said below
- kernel: bfloat16 [27, 256], replicated, may hold values from -1.25 to 1.25
- mix_weight: bfloat16 [4, 64, 64], replicated, may hold values from -0.75 to 0.75
- norm_gain: float32 [256], replicated, may hold values from 0.25 to 1.75
- upstream: bfloat16 [128, 16, 128, 256], P('gx', 'gy'), may hold values from -6 to 6
Outputs:
- output: bfloat16 [128, 16, 128, 256], P('gx', 'gy')
- volume_grad: bfloat16 [128, 16, 128, 256], P('gx', 'gy')
- kernel_grad: float32 [27, 256], replicated
- mix_grad: float32 [4, 64, 64], replicated
Inputs may be any that keep to these rules, and one draw needn't show every extreme that they name: `void_mask`: 1 marks a void voxel; voxels whose third index is a multiple of 8 are never void.
All inputs are finite; a program needn't handle non-finite values.
Results may differ from a plain program's by a relative error of at most 0.0017.
The roundings to bfloat16 on the way count: a program that leaves them out, or rounds other values in their place, can miss the bound.
Values may be sent and summed in bfloat16 or wider, within the bound.
No kernel may reach another device: no remote copies, remote signals or barrier semaphores. Data moves between devices by JAX's collectives and lax.ppermute only.
A program may use at most 128 MiB of HBM per device.

v0:
```python
import jax
import jax.numpy as jnp
from jax import lax
from jax.sharding import PartitionSpec as P

SWEEPS = 5
HI = lax.Precision.HIGHEST
EPS = 1e-05


def padded_2(block, sides, width):
    for axis, dim in sides:
        count = lax.axis_size(axis)
        forward = [(i, i + 1) for i in range(count - 1)]
        forward.append((count - 1, 0))
        backward = [(target, source) for source, target in forward]
        low = lax.ppermute(
            lax.slice_in_dim(block, block.shape[dim] - width, None, axis=dim), axis, forward
        )
        high = lax.ppermute(lax.slice_in_dim(block, 0, width, axis=dim), axis, backward)
        block = jnp.concatenate([low, block, high], axis=dim)
    return block


def whiten(sigma):
    eye = jnp.eye(sigma.shape[0], dtype=sigma.dtype)
    trace = jnp.trace(sigma)
    scaled = sigma / trace
    proj = eye
    for sweep in range(SWEEPS):
        cube = jnp.dot(
            proj, jnp.dot(proj, jnp.dot(proj, scaled, precision=HI), precision=HI), precision=HI
        )
        proj = 1.5 * proj - 0.5 * cube
    return proj / jnp.sqrt(trace)


def sigma_back(sigma, dwhite):
    return jax.vjp(whiten, sigma)[1](dwhite)[0]


def zwrap(field):
    return jnp.concatenate([field[:, :, -1:], field, field[:, :, :1]], axis=2)


def stencil(padded, kernel, flip):
    size_x, size_y, depth = (padded.shape[0] - 2, padded.shape[1] - 2, padded.shape[2] - 2)
    taps = kernel.astype(jnp.float32)
    total = jnp.zeros((size_x, size_y, depth, padded.shape[3]), jnp.float32)
    for tap in range(27):
        ox, oy, oz = (tap // 9, tap // 3 % 3, tap % 3)
        if flip:
            ox, oy, oz = (2 - ox, 2 - oy, 2 - oz)
        piece = padded[ox : ox + size_x, oy : oy + size_y, oz : oz + depth]
        total = total + piece.astype(jnp.float32) * taps[tap]
    return total


def inner(field, edge):
    return field[edge : field.shape[0] - edge, edge : field.shape[1] - edge]


def per_device(volume, void_mask, kernel, mix_weight, norm_gain, upstream):
    size_x, size_y, depth, chans = volume.shape
    groups, width = (mix_weight.shape[0], mix_weight.shape[1])
    scale = jnp.float32(size_x * size_y * depth * lax.axis_size("gx") * lax.axis_size("gy"))
    keep_own = (1 - void_mask).astype(jnp.float32)
    rim = 1
    padded_x = padded_2(volume, (("gx", 0), ("gy", 1)), 1)
    edge = rim - 1
    padded_z = zwrap(padded_x)
    field = lax.optimization_barrier(stencil(padded_z, kernel, False).astype(jnp.bfloat16)).astype(
        jnp.float32
    )
    ext_x, ext_y = (field.shape[0], field.shape[1])
    field_own = inner(field, edge)
    masked_own = keep_own[..., None] * field_own
    count_part = jnp.sum(keep_own)
    sum_part = jnp.sum(masked_own, axis=(0, 1, 2))
    eye = jnp.eye(width, dtype=jnp.float32)
    count, total = lax.psum((count_part, sum_part), ("gx", "gy"))
    mean = (total / count).reshape(groups, width)
    cent_own = field_own.reshape(size_x, size_y, depth, groups, width) - mean
    cov_part = jnp.einsum(
        "abzgi,abzgj->gij", keep_own[..., None, None] * cent_own, cent_own, precision=HI
    )
    sigma = lax.psum(cov_part, ("gx", "gy")) / count + EPS * eye
    white = jax.vmap(whiten)(sigma)
    centered = field.reshape(ext_x, ext_y, depth, groups, width) - mean
    gain = norm_gain.reshape(groups, width)
    pre = jnp.einsum("abzgj,gij->abzgi", centered, white, precision=HI) * gain
    active = jax.nn.silu(pre).astype(jnp.bfloat16)
    active_own = inner(active, edge)
    grad_five = upstream.reshape(ext_x, ext_y, depth, groups, width)
    mixed = jnp.einsum(
        "abzgi,gio->abzgo", active_own, mix_weight, preferred_element_type=jnp.float32
    )
    output = (volume.astype(jnp.float32) + mixed.reshape(size_x, size_y, depth, chans)).astype(
        jnp.bfloat16
    )
    dact = jnp.einsum("abzgo,gio->abzgi", grad_five, mix_weight, preferred_element_type=jnp.float32)
    sig = jax.nn.sigmoid(pre)
    dnormed = dact * sig * (1.0 + pre * (1.0 - sig)) * gain
    dcent = jnp.einsum("abzgi,gij->abzgj", dnormed, white, precision=HI)
    dwhite_part = jnp.einsum(
        "abzgi,abzgj->gij", inner(dnormed, edge), inner(centered, edge), precision=HI
    )
    dsum_part = jnp.sum(inner(dcent, edge), axis=(0, 1, 2))
    dwhite, dsum = lax.psum((dwhite_part, dsum_part), ("gx", "gy"))
    sens = jax.vmap(sigma_back)(sigma, dwhite)
    sym = sens + jnp.swapaxes(sens, 1, 2)
    dfield = dcent + keep_own[..., None, None] / count * (
        jnp.einsum("abzgj,gjk->abzgk", centered, sym, precision=HI) - dsum
    )
    dfield = lax.optimization_barrier(
        dfield.astype(jnp.bfloat16).reshape(ext_x, ext_y, depth, chans)
    )
    dfield_pad = zwrap(padded_2(dfield, (("gx", 0), ("gy", 1)), 1))
    back = stencil(dfield_pad, kernel, True)
    volume_grad = (upstream.astype(jnp.float32) + back).astype(jnp.bfloat16)
    dfield_own = inner(dfield, edge).astype(jnp.float32)
    ker_terms = []
    for tap in range(27):
        ox, oy, oz = (tap // 9, tap // 3 % 3, tap % 3)
        piece = padded_z[
            edge + ox : edge + ox + size_x, edge + oy : edge + oy + size_y, oz : oz + depth
        ]
        ker_terms.append(jnp.sum(piece.astype(jnp.float32) * dfield_own, axis=(0, 1, 2)))
    ker_part = jnp.stack(ker_terms)
    mix_part = jnp.einsum(
        "abzgi,abzgo->gio",
        active_own,
        upstream.reshape(size_x, size_y, depth, groups, width),
        preferred_element_type=jnp.float32,
    )
    ker_sum, mix_sum = lax.psum((ker_part, mix_part), ("gx", "gy"))
    return (output, volume_grad, ker_sum / scale, mix_sum / scale)


def solution(mesh):
    in_specs = (
        P("gx", "gy", None, None),
        P("gx", "gy", None),
        P(),
        P(),
        P(),
        P("gx", "gy", None, None),
    )
    out_specs = (P("gx", "gy", None, None), P("gx", "gy", None, None), P(), P())
    return jax.shard_map(
        per_device, mesh=mesh, in_specs=in_specs, out_specs=out_specs, check_vma=False
    )
```

profile of v0, /device:TPU:32, one launch (start us, length us, event | category | flops | bytes accessed | tf_op | source)
XLA Modules:
  0.0 774.9 jit_solution(11708608485674876713)
XLA Ops:
  7.3 1.4 copy.36
  8.8 3.8 collective-permute-start.1
  14.0 1.5 fusion.156
  15.5 1.2 collective-permute-done
  16.8 1.7 collective-permute-start.2
  18.4 1.7 collective-permute-start.3
  21.4 1.1 copy.47
  22.6 3.5 collective-permute-done.2
  27.5 5.9 maximum_maximum_fusion
  33.7 4.6 fusion.47
  39.3 79.1 %all-reduce = (f32[256]{0:T(256)S(1)}, f32[]{:T(128)}) all-reduce(f32[256]{0:T(256)S(1)} %multiply_reduce_fusion, f32[]{:T(128)} %fusion.150), channel_id=1, replica_groups=mesh['gx'=64,'gy'=4] {'gx','gy'}, use_global_device_ids=true, to_apply=%region_1.0 | all-reduce | flops 257 | bytes 2056 | tf_op jit(solution)/shard_map/psum | solution.py:81
  119.1 3.2 fusion.10
  122.8 1.2 broadcast_divide_fusion.7
  124.1 235.6 %all-reduce.5.cloned.1.call-done = f32[4,64,64]{2,1,0:T(8,128)} async-done(((f32[4,64,64]{2,1,0:T(8,128)}), f32[4,64,64]{2,1,0:T(8,128)}) %all-reduce.5.cloned.1.call-update) | async-done | bytes 65552 | tf_op jit(solution)/shard_map/psum | solution.py:87
  359.7 1.7 select_reduce_fusion
  362.0 1.6 broadcast_divide_fusion.2
  369.2 2.0 multiply_convert_fusion
  371.8 1.8 convolution_bitcast_fusion.6
  373.6 2.1 fusion.157
  376.7 1.4 convolution_bitcast_fusion.1
  378.1 1.1 copy.46
  379.2 76.3 %psum.53 = f32[4,64]{1,0:T(4,128)S(1)} all-reduce(f32[4,64]{1,0:T(4,128)S(1)} %get-tuple-element.105), channel_id=1, replica_groups=mesh['gx'=64,'gy'=4] {'gx','gy'}, use_global_device_ids=true, to_apply=%region_10.11 | all-reduce | flops 256 | bytes 2048 | tf_op jit(solution)/shard_map/psum | solution.py:109
  455.5 168.1 %all-reduce.7.cloned.1.call-done = (f32[4,64,64]{2,1,0:T(8,128)}, f32[4,64,64]{2,1,0:T(8,128)}) async-done(((f32[4,64,64]{2,1,0:T(8,128)}, f32[4,64,64]{2,1,0:T(8,128)}), (f32[4,64,64]{2,1,0:T(8,128)}, f32[4,64,64]{2,1,0:T(8,128)})) %all-reduce.7.cloned.1.call-update) | async-done | bytes 131088 | tf_op jit(solution)/shard_map/psum | solution.py:109
  623.6 1.5 fusion.114
  625.1 1.5 convolution_add_fusion.14
  626.5 1.2 fusion.166
  627.7 1.2 fusion.167
  628.9 1.3 convolution_add_fusion.13
  638.2 1.7 copy.71
  639.8 1.4 convolution_add_fusion.1
  641.3 1.3 fusion.16
  643.9 1.7 copy.70
  645.6 2.5 multiply_reduce_fusion.1
  648.2 2.9 fusion.9
  652.8 3.4 collective-permute-start.5
  656.2 4.8 fusion.90
  661.0 1.5 fusion.89
  662.6 78.1 %psum.54 = f32[27,256]{1,0:T(8,128)S(1)} all-reduce(f32[27,256]{1,0:T(8,128)S(1)} %stack.111), channel_id=1, replica_groups=mesh['gx'=64,'gy'=4] {'gx','gy'}, use_global_device_ids=true, to_apply=%region_38.39 | all-reduce | flops 6912 | bytes 55296 | tf_op jit(solution)/shard_map/psum | solution.py:136
  740.7 1.1 pad_maximum_fusion.12
  741.9 3.2 collective-permute-start.7
  745.8 2.0 copy.76
  747.8 1.6 broadcast_multiply_fusion
  749.4 1.3 collective-permute-done.6
  750.7 1.4 pad_maximum_fusion.3
  752.8 1.6 pad_maximum_fusion.5
  754.6 4.6 pad_maximum_fusion.1
  759.5 6.3 fusion.93
  765.8 2.0 copy.77
  (302 shorter events, 26.2 us)
Async XLA Ops:
  7.2 364.1 %copy-start = (bf16[4,64,64]{2,1,0:T(8,128)(2,1)S(1)}, bf16[4,64,64]{2,1,0:T(8,128)(2,1)}, u32[]{:S(2)}) copy-start(bf16[4,64,64]{2,1,0:T(8,128)(2,1)} %param.9) | copy-start | bytes 98308
  7.2 12.9 %copy-start.49 = (s32[2,4,128]{2,1,0:T(4,128)S(1)}, s32[2,4,128]{2,1,0:T(4,128)}, u32[]{:S(2)}) copy-start(s32[2,4,128]{2,1,0:T(4,128)} %param.7) | copy-start | bytes 12292
  7.2 15.2 %copy-start.48 = (bf16[27,256]{1,0:T(8,128)(2,1)S(1)}, bf16[27,256]{1,0:T(8,128)(2,1)}, u32[]{:S(2)}) copy-start(bf16[27,256]{1,0:T(8,128)(2,1)} %param.8) | copy-start | bytes 41476
  7.2 13.5 %copy-start.114 = (f32[256]{0:T(256)S(1)}, f32[256]{0:T(256)}, u32[]{:S(2)}) copy-start(f32[256]{0:T(256)} %param.10) | copy-start | bytes 3076
  7.2 14.1 %copy-start.47 = (bf16[2,4,128,256]{3,2,1,0:T(8,128)(2,1)S(1)}, bf16[2,4,128,256]{3,2,1,0:T(8,128)(2,1)}, u32[]{:S(2)}) copy-start(bf16[2,4,128,256]{3,2,1,0:T(8,128)(2,1)} %param.11) | copy-start | bytes 1572868
  7.2 352.5 %all-reduce.5.cloned.1.call-start = ((), (), s32[]{:S(2)}) async-start(), calls=%async_computation | async-start | bytes 262144 | tf_op jit(solution)/shard_map/psum | solution.py:87
  8.7 18.4 %copy-start.5 = (bf16[2,4,128,256]{2,3,1,0:T(8,128)(2,1)}, bf16[2,4,128,256]{2,3,1,0:T(8,128)(2,1)S(1)}, u32[]{:S(2)}) copy-start(bf16[2,4,128,256]{2,3,1,0:T(8,128)(2,1)S(1)} %copy.36) | copy-start | bytes 1572868
  8.7 8.0 %collective-permute-start = (bf16[1,4,128,256]{2,3,1,0:T(8,128)(2,1)S(1)}, bf16[1,4,128,256]{2,3,1,0:T(8,128)(2,1)S(1)}, u32[]{:S(2)}, u32[]{:S(2)}) collective-permute-start(bf16[1,4,128,256]{2,3,1,0:T(8,128)(2,1)S(1)} %get-tuple-element.74), channel_id=1, source_target_pairs={{0,4},{4,8},{8,12},{12,16},{16,20},{20,24},{24,28},{28,32},{32,36}... | collective-permute-start | bytes 786440 | tf_op jit(solution)/shard_map/ppermute | solution.py:17
  8.8 7.9 %collective-permute-start.1 = (bf16[1,4,128,256]{2,3,1,0:T(8,128)(2,1)S(1)}, bf16[1,4,128,256]{2,3,1,0:T(8,128)(2,1)S(1)}, u32[]{:S(2)}, u32[]{:S(2)}) collective-permute-start(bf16[1,4,128,256]{2,3,1,0:T(8,128)(2,1)S(1)} %get-tuple-element.73), channel_id=1, source_target_pairs={{4,0},{8,4},{12,8},{16,12},{20,16},{24,20},{28,24},{32,28},{36,32}... | collective-permute-start | bytes 786440 | tf_op jit(solution)/shard_map/ppermute | solution.py:20
  13.4 24.9 %copy-start.52 = (f32[2,4,128]{2,1,0:T(4,128)}, f32[2,4,128]{2,1,0:T(4,128)S(1)}, u32[]{:S(2)}) copy-start(f32[2,4,128]{2,1,0:T(4,128)S(1)} %subtract_convert_fusion) | copy-start | bytes 12292
  16.7 16.7 %copy-start.12 = (bf16[1,4,128,256]{2,3,1,0:T(8,128)(2,1)}, bf16[1,4,128,256]{2,3,1,0:T(8,128)(2,1)S(1)}, u32[]{:S(2)}) copy-start(bf16[1,4,128,256]{2,3,1,0:T(8,128)(2,1)S(1)} %collective-permute-done) | copy-start | bytes 786436
  16.8 9.3 %collective-permute-start.2 = (bf16[4,1,128,256]{2,3,1,0:T(8,128)(2,1)S(1)}, bf16[4,1,128,256]{2,3,1,0:T(8,128)(2,1)S(1)}, u32[]{:S(2)}, u32[]{:S(2)}) collective-permute-start(bf16[4,1,128,256]{2,3,1,0:T(8,128)(2,1)S(1)} %get-tuple-element.68), channel_id=1, source_target_pairs={{0,1},{1,2},{2,3},{3,0},{4,5},{5,6},{6,7},{7,4},{8,9},{9,10},{10,1... | collective-permute-start | bytes 786440 | tf_op jit(solution)/shard_map/ppermute | solution.py:17
  18.4 7.7 collective-permute-start.3
  22.4 11.0 %copy-start.71 = (f32[1,256]{1,0:T(1,128)}, f32[1,256]{1,0:T(1,128)S(1)}, u32[]{:S(2)}) copy-start(f32[1,256]{1,0:T(1,128)S(1)} %get-tuple-element.75) | copy-start | bytes 3076
  22.4 11.0 %copy-start.73 = (f32[1,256]{1,0:T(1,128)}, f32[1,256]{1,0:T(1,128)S(1)}, u32[]{:S(2)}) copy-start(f32[1,256]{1,0:T(1,128)S(1)} %get-tuple-element.76) | copy-start | bytes 3076
  22.5 11.0 %copy-start.75 = (f32[1,256]{1,0:T(1,128)}, f32[1,256]{1,0:T(1,128)S(1)}, u32[]{:S(2)}) copy-start(f32[1,256]{1,0:T(1,128)S(1)} %get-tuple-element.77) | copy-start | bytes 3076
  22.5 11.0 %copy-start.77 = (f32[1,256]{1,0:T(1,128)}, f32[1,256]{1,0:T(1,128)S(1)}, u32[]{:S(2)}) copy-start(f32[1,256]{1,0:T(1,128)S(1)} %get-tuple-element.78) | copy-start | bytes 3076
  22.5 11.0 %copy-start.79 = (f32[1,256]{1,0:T(1,128)}, f32[1,256]{1,0:T(1,128)S(1)}, u32[]{:S(2)}) copy-start(f32[1,256]{1,0:T(1,128)S(1)} %get-tuple-element.79) | copy-start | bytes 3076
  22.5 11.0 %copy-start.81 = (f32[1,256]{1,0:T(1,128)}, f32[1,256]{1,0:T(1,128)S(1)}, u32[]{:S(2)}) copy-start(f32[1,256]{1,0:T(1,128)S(1)} %get-tuple-element.80) | copy-start | bytes 3076
  22.5 11.0 %copy-start.83 = (f32[1,256]{1,0:T(1,128)}, f32[1,256]{1,0:T(1,128)S(1)}, u32[]{:S(2)}) copy-start(f32[1,256]{1,0:T(1,128)S(1)} %get-tuple-element.81) | copy-start | bytes 3076
  22.5 11.0 %copy-start.85 = (f32[1,256]{1,0:T(1,128)}, f32[1,256]{1,0:T(1,128)S(1)}, u32[]{:S(2)}) copy-start(f32[1,256]{1,0:T(1,128)S(1)} %get-tuple-element.82) | copy-start | bytes 3076
  22.5 11.0 %copy-start.87 = (f32[1,256]{1,0:T(1,128)}, f32[1,256]{1,0:T(1,128)S(1)}, u32[]{:S(2)}) copy-start(f32[1,256]{1,0:T(1,128)S(1)} %get-tuple-element.83) | copy-start | bytes 3076
  22.5 11.0 %copy-start.89 = (f32[1,256]{1,0:T(1,128)}, f32[1,256]{1,0:T(1,128)S(1)}, u32[]{:S(2)}) copy-start(f32[1,256]{1,0:T(1,128)S(1)} %get-tuple-element.84) | copy-start | bytes 3076
  22.5 11.0 %copy-start.91 = (f32[1,256]{1,0:T(1,128)}, f32[1,256]{1,0:T(1,128)S(1)}, u32[]{:S(2)}) copy-start(f32[1,256]{1,0:T(1,128)S(1)} %get-tuple-element.85) | copy-start | bytes 3076
  22.6 11.0 %copy-start.93 = (f32[1,256]{1,0:T(1,128)}, f32[1,256]{1,0:T(1,128)S(1)}, u32[]{:S(2)}) copy-start(f32[1,256]{1,0:T(1,128)S(1)} %get-tuple-element.86) | copy-start | bytes 3076
  22.6 11.0 %copy-start.95 = (f32[1,256]{1,0:T(1,128)}, f32[1,256]{1,0:T(1,128)S(1)}, u32[]{:S(2)}) copy-start(f32[1,256]{1,0:T(1,128)S(1)} %get-tuple-element.87) | copy-start | bytes 3076
  22.6 11.0 %copy-start.97 = (f32[1,256]{1,0:T(1,128)}, f32[1,256]{1,0:T(1,128)S(1)}, u32[]{:S(2)}) copy-start(f32[1,256]{1,0:T(1,128)S(1)} %get-tuple-element.88) | copy-start | bytes 3076
  22.6 11.0 %copy-start.99 = (f32[1,256]{1,0:T(1,128)}, f32[1,256]{1,0:T(1,128)S(1)}, u32[]{:S(2)}) copy-start(f32[1,256]{1,0:T(1,128)S(1)} %get-tuple-element.89) | copy-start | bytes 3076
  22.6 11.0 %copy-start.101 = (f32[1,256]{1,0:T(1,128)}, f32[1,256]{1,0:T(1,128)S(1)}, u32[]{:S(2)}) copy-start(f32[1,256]{1,0:T(1,128)S(1)} %get-tuple-element.90) | copy-start | bytes 3076
  22.6 11.0 %copy-start.103 = (f32[1,256]{1,0:T(1,128)}, f32[1,256]{1,0:T(1,128)S(1)}, u32[]{:S(2)}) copy-start(f32[1,256]{1,0:T(1,128)S(1)} %get-tuple-element.91) | copy-start | bytes 3076
  22.6 11.0 %copy-start.105 = (f32[1,256]{1,0:T(1,128)}, f32[1,256]{1,0:T(1,128)S(1)}, u32[]{:S(2)}) copy-start(f32[1,256]{1,0:T(1,128)S(1)} %get-tuple-element.92) | copy-start | bytes 3076
  22.6 11.0 %copy-start.107 = (f32[1,256]{1,0:T(1,128)}, f32[1,256]{1,0:T(1,128)S(1)}, u32[]{:S(2)}) copy-start(f32[1,256]{1,0:T(1,128)S(1)} %get-tuple-element.93) | copy-start | bytes 3076
  122.3 501.2 %all-reduce.7.cloned.1.call-start = ((), (), s32[]{:S(2)}) async-start(), calls=%async_computation.1 | async-start | bytes 524288 | tf_op jit(solution)/shard_map/psum | solution.py:109
  362.0 11.6 %copy-start.112 = (f32[4]{0:T(128)}, f32[4]{0:T(128)S(1)}, u32[]{:S(2)}) copy-start(f32[4]{0:T(128)S(1)} %get-tuple-element.104) | copy-start | bytes 52
  375.7 247.8 %copy-start.113 = (f32[4]{0:T(128)S(1)}, f32[4]{0:T(128)}, u32[]{:S(2)}) copy-start(f32[4]{0:T(128)} %copy-done.112) | copy-start | bytes 52
  633.5 12.1 %copy-start.109 = (f32[4]{0:T(128)S(1)}, f32[4]{0:T(128)}, u32[]{:S(2)}) copy-start(f32[4]{0:T(128)} %get-tuple-element.102) | copy-start | bytes 52
  633.5 12.1 %copy-start.110 = (f32[4]{0:T(128)S(1)}, f32[4]{0:T(128)}, u32[]{:S(2)}) copy-start(f32[4]{0:T(128)} %get-tuple-element.103) | copy-start | bytes 52
  633.9 14.2 %copy-start.54 = (f32[4]{0:T(128)S(1)}, f32[4]{0:T(128)}, u32[]{:S(2)}) copy-start(f32[4]{0:T(128)} %copy-done.53) | copy-start | bytes 52
  633.9 14.3 %copy-start.50 = (pred[64,64]{1,0:T(8,128)(4,1)S(1)}, pred[64,64]{1,0:T(8,128)(4,1)}, u32[]{:S(2)}) copy-start(pred[64,64]{1,0:T(8,128)(4,1)} %iota_compare_fusion) | copy-start | bytes 12292
  634.0 14.2 %copy-start.51 = (f32[2,4,128]{2,1,0:T(4,128)S(1)}, f32[2,4,128]{2,1,0:T(4,128)}, u32[]{:S(2)}) copy-start(f32[2,4,128]{2,1,0:T(4,128)} %broadcast_divide_fusion.7) | copy-start | bytes 12292
  642.9 13.3 %copy-start.13 = (bf16[1,4,128,256]{2,3,1,0:T(8,128)(2,1)S(1)}, bf16[1,4,128,256]{2,3,1,0:T(8,128)(2,1)}, u32[]{:S(2)}) copy-start(bf16[1,4,128,256]{2,3,1,0:T(8,128)(2,1)} %copy-done.12) | copy-start | bytes 786436
  645.6 10.6 %copy-start.11 = (bf16[4,5,128,256]{2,3,1,0:T(8,128)(2,1)S(1)}, bf16[4,5,128,256]{2,3,1,0:T(8,128)(2,1)}, u32[]{:S(2)}) copy-start(bf16[4,5,128,256]{2,3,1,0:T(8,128)(2,1)} %copy-done.10) | copy-start | bytes 3932164
  645.6 10.6 %copy-start.16 = (bf16[1,4,128,256]{2,3,1,0:T(8,128)(2,1)S(1)}, bf16[1,4,128,256]{2,3,1,0:T(8,128)(2,1)}, u32[]{:S(2)}) copy-start(bf16[1,4,128,256]{2,3,1,0:T(8,128)(2,1)} %copy-done.14) | copy-start | bytes 786436
  652.1 88.6 %collective-permute-start.4 = (bf16[1,4,128,256]{2,3,1,0:T(8,128)(2,1)}, bf16[1,4,128,256]{2,3,1,0:T(8,128)(2,1)}, u32[]{:S(2)}, u32[]{:S(2)}) collective-permute-start(bf16[1,4,128,256]{2,3,1,0:T(8,128)(2,1)} %get-tuple-element.71), channel_id=1, source_target_pairs={{0,4},{4,8},{8,12},{12,16},{16,20},{20,24},{24,28},{28,32},{32,36}... | collective-permute-start | bytes 786440 | tf_op jit(solution)/shard_map/ppermute | solution.py:17
  652.8 87.9 %collective-permute-start.5 = (bf16[1,4,128,256]{2,3,1,0:T(8,128)(2,1)}, bf16[1,4,128,256]{2,3,1,0:T(8,128)(2,1)}, u32[]{:S(2)}, u32[]{:S(2)}) collective-permute-start(bf16[1,4,128,256]{2,3,1,0:T(8,128)(2,1)} %get-tuple-element.72), channel_id=1, source_target_pairs={{4,0},{8,4},{12,8},{16,12},{20,16},{24,20},{28,24},{32,28},{36,32}... | collective-permute-start | bytes 786440 | tf_op jit(solution)/shard_map/ppermute | solution.py:20
  662.5 88.2 %copy-start.4 = (bf16[2,4,128,4,64]{2,4,3,1,0:T(8,128)(2,1)S(1)}, bf16[2,4,128,4,64]{2,4,3,1,0:T(8,128)(2,1)}, u32[]{:S(2)}) copy-start(bf16[2,4,128,4,64]{2,4,3,1,0:T(8,128)(2,1)} %copy-done.3) | copy-start | bytes 1572868
  741.8 8.8 %collective-permute-start.6 = (bf16[4,1,128,256]{2,3,1,0:T(8,128)(2,1)S(1)}, bf16[4,1,128,256]{2,3,1,0:T(8,128)(2,1)S(1)}, u32[]{:S(2)}, u32[]{:S(2)}) collective-permute-start(bf16[4,1,128,256]{2,3,1,0:T(8,128)(2,1)S(1)} %get-tuple-element.64), channel_id=1, source_target_pairs={{0,1},{1,2},{2,3},{3,0},{4,5},{5,6},{6,7},{7,4},{8,9},{9,10},{10,1... | collective-permute-start | bytes 786440 | tf_op jit(solution)/shard_map/ppermute | solution.py:17
  741.9 8.7 %collective-permute-start.7 = (bf16[4,1,128,256]{2,3,1,0:T(8,128)(2,1)S(1)}, bf16[4,1,128,256]{2,3,1,0:T(8,128)(2,1)S(1)}, u32[]{:S(2)}, u32[]{:S(2)}) collective-permute-start(bf16[4,1,128,256]{2,3,1,0:T(8,128)(2,1)S(1)} %get-tuple-element.65), channel_id=1, source_target_pairs={{1,0},{2,1},{3,2},{0,3},{5,4},{6,5},{7,6},{4,7},{9,8},{10,9},{11,1... | collective-permute-start | bytes 786440 | tf_op jit(solution)/shard_map/ppermute | solution.py:20
  (77 other events, 374.8 us)
Sparse Core Ops, SparseCore 0:
  122.5 237.1 all-reduce.4
  376.8 246.6 all-reduce.6
where the time goes:
time: 783 us; the launch traced here: 775 us
  waiting for transfers between devices  410 us (52%)
  blocking collectives  233 us (30%)
  other arithmetic  44.9 us (6%)
  matrix products  36.3 us (5%)
  local copies, waits for them, and re-layouts  19.2 us (2%)
  between operations  16.2 us (2%)
  starting transfers between devices  15.1 us (2%)
    psum x1, waiting for transfers between devices, per_device(): sigma = lax.psum(cov_part, ('gx', 'gy')) / count + EPS * eye  236 us
    psum x1, waiting for transfers between devices, per_device(): dwhite, dsum = lax.psum((dwhite_part, dsum_part), ('gx', 'gy'))  168 us
    psum x1, blocking collectives, per_device(): count, total = lax.psum((count_part, sum_part), ('gx', 'gy'))  79.1 us
    psum x1, blocking collectives, per_device(): ker_sum, mix_sum = lax.psum((ker_part, mix_part), ('gx', 'gy'))  78.1 us
    psum x1, blocking collectives, per_device(): dwhite, dsum = lax.psum((dwhite_part, dsum_part), ('gx', 'gy'))  76.3 us
  transfers between devices with their start and end apart: 10, of which 5 were waited for; matrix products, arithmetic and copies ran while one was open for 3% of the time, Pallas kernels for 0%

commit v1 on v0

--- a/solution.py
+++ b/solution.py
@@ -84,7 +84,7 @@
     cov_part = jnp.einsum(
         "abzgi,abzgj->gij", keep_own[..., None, None] * cent_own, cent_own, precision=HI
     )
-    sigma = lax.psum(cov_part, ("gx", "gy")) / count + EPS * eye
+    sigma = jnp.sum(lax.all_gather(cov_part, ("gx", "gy")), axis=0) / count + EPS * eye
     white = jax.vmap(whiten)(sigma)
     centered = field.reshape(ext_x, ext_y, depth, groups, width) - mean
     gain = norm_gain.reshape(groups, width)

time: 783 us -> 707 us (0.903)
  waiting for transfers between devices: 410 us -> 320 us
    psum x1 -> x0, waiting for transfers between devices: 236 us -> none  [per_device(): sigma = lax.psum(cov_part, ('gx', 'gy')) / count + EPS * eye]
    all_gather x0 -> x1, waiting for transfers between devices: none -> 142 us  [per_device(): lax.all_gather(cov_part, ('gx', 'gy'))]
    reduce_sum x1 -> x2, other arithmetic: 2.54 us -> 12.5 us  [the longest x1 12.3 us: per_device(): jnp.sum(lax.all_gather(cov_part, ('gx', 'gy')), axis=0) / count + EPS * eye]
where the time goes in v1:
time: 707 us; the launch traced here: 699 us
  waiting for transfers between devices  320 us (45%)
  blocking collectives  234 us (33%)
  other arithmetic  52.6 us (7%)
  matrix products  41.9 us (6%)
  local copies, waits for them, and re-layouts  19 us (3%)
  between operations  16.2 us (2%)
  starting transfers between devices  15.1 us (2%)
    psum x1, waiting for transfers between devices, per_device(): dwhite, dsum = lax.psum((dwhite_part, dsum_part), ('gx', 'gy'))  169 us
    all_gather x1, waiting for transfers between devices, per_device(): lax.all_gather(cov_part, ('gx', 'gy'))  142 us
    psum x1, blocking collectives, per_device(): count, total = lax.psum((count_part, sum_part), ('gx', 'gy'))  79.1 us
    psum x1, blocking collectives, per_device(): ker_sum, mix_sum = lax.psum((ker_part, mix_part), ('gx', 'gy'))  78.1 us
    psum x1, blocking collectives, per_device(): dwhite, dsum = lax.psum((dwhite_part, dsum_part), ('gx', 'gy'))  76.9 us
  transfers between devices with their start and end apart: 10, of which 5 were waited for; matrix products, arithmetic and copies ran while one was open for 3% of the time, Pallas kernels for 0%

profile of v1, /device:TPU:32, one launch (start us, length us, event | category | flops | bytes accessed | tf_op | source)
XLA Modules:
  0.0 698.7 jit_solution(6259132379625540567)
XLA Ops:
  7.3 1.3 copy.86
  8.7 3.8 collective-permute-start.1
  14.2 2.4 collective-permute-done
  16.7 1.7 collective-permute-start.2
  18.3 1.7 collective-permute-start.3
  20.8 5.2 collective-permute-done.2
  27.3 5.1 maximum_maximum_fusion
  32.7 4.6 fusion.47
  38.3 79.1 %all-reduce = (f32[256]{0:T(256)S(1)}, f32[]{:T(128)}) all-reduce(f32[256]{0:T(256)S(1)} %multiply_reduce_fusion, f32[]{:T(128)} %fusion.150), channel_id=1, replica_groups=mesh['gx'=64,'gy'=4] {'gx','gy'}, use_global_device_ids=true, to_apply=%region_1.0 | all-reduce | flops 257 | bytes 2056 | tf_op jit(solution)/shard_map/psum | solution.py:81
  118.1 3.2 fusion.10
  122.8 2.1 copy.103
  125.4 1.3 broadcast_divide_fusion.7
  126.7 142.1 %all-gather.3.cloned.1.call-done = f32[1024,64,64]{2,1,0:T(8,128)} async-done(((f32[4,64,64]{2,1,0:T(8,128)}), f32[1024,64,64]{2,1,0:T(8,128)}) %all-gather.3.cloned.1.call-update) | async-done | bytes 16777232 | tf_op jit(solution)/shard_map/all_gather | solution.py:87
  268.8 12.3 %reduce_sum.314 = f32[4,64,64]{2,1,0:T(8,128)S(1)} reduce(f32[256,4,64,64]{3,2,1,0:T(8,128)} %bitcast.241, f32[]{:T(128)} %constant.12.clone.1), dimensions={0}, to_apply=%region_4.0 | reduce | flops 4177920 | bytes 16842756 | tf_op jit(solution)/shard_map/reduce_sum | solution.py:87
  289.4 1.3 multiply_convert_fusion
  291.3 1.9 convolution_bitcast_fusion.6
  293.1 2.1 fusion.157
  296.2 1.4 convolution_bitcast_fusion.1
  298.7 76.9 %psum.45 = f32[4,64]{1,0:T(4,128)S(1)} all-reduce(f32[4,64]{1,0:T(4,128)S(1)} %get-tuple-element.109), channel_id=1, replica_groups=mesh['gx'=64,'gy'=4] {'gx','gy'}, use_global_device_ids=true, to_apply=%region_10.11 | all-reduce | flops 256 | bytes 2048 | tf_op jit(solution)/shard_map/psum | solution.py:109
  375.6 168.7 %all-reduce.4.cloned.1.call-done = (f32[4,64,64]{2,1,0:T(8,128)}, f32[4,64,64]{2,1,0:T(8,128)}) async-done(((f32[4,64,64]{2,1,0:T(8,128)}, f32[4,64,64]{2,1,0:T(8,128)}), (f32[4,64,64]{2,1,0:T(8,128)}, f32[4,64,64]{2,1,0:T(8,128)})) %all-reduce.4.cloned.1.call-update) | async-done | bytes 131088 | tf_op jit(solution)/shard_map/psum | solution.py:109
  544.3 1.5 convolution_add_fusion.14
  545.8 1.5 fusion.114
  547.2 1.2 fusion.166
  548.4 1.3 convolution_add_fusion.13
  550.2 1.3 convolution_add_fusion.10
  551.5 1.3 fusion.113
  552.8 1.2 fusion.168
  553.9 1.3 convolution_add_fusion.9
  555.7 1.3 convolution_add_fusion.6
  556.9 1.3 fusion.112
  558.2 1.2 fusion.169
  565.7 1.7 copy.130
  567.5 2.6 multiply_reduce_fusion.1
  570.0 1.6 copy.131
  571.7 3.0 fusion.9
  576.4 3.4 collective-permute-start.5
  579.8 5.1 fusion.90
  584.9 1.5 fusion.89
  586.5 78.1 %psum.46 = f32[27,256]{1,0:T(8,128)S(1)} all-reduce(f32[27,256]{1,0:T(8,128)S(1)} %stack.111), channel_id=1, replica_groups=mesh['gx'=64,'gy'=4] {'gx','gy'}, use_global_device_ids=true, to_apply=%region_38.39 | all-reduce | flops 6912 | bytes 55296 | tf_op jit(solution)/shard_map/psum | solution.py:136
  665.8 3.2 collective-permute-start.7
  669.7 2.0 copy.136
  671.7 1.6 broadcast_multiply_fusion
  673.3 1.3 collective-permute-done.6
  674.5 1.4 pad_maximum_fusion.3
  676.6 1.6 pad_maximum_fusion.5
  678.5 4.6 pad_maximum_fusion.1
  683.3 6.3 fusion.93
  689.6 2.0 copy.137
  (294 shorter events, 29.4 us)
Async XLA Ops:
  7.2 283.6 %copy-start = (bf16[4,64,64]{2,1,0:T(8,128)(2,1)S(1)}, bf16[4,64,64]{2,1,0:T(8,128)(2,1)}, u32[]{:S(2)}) copy-start(bf16[4,64,64]{2,1,0:T(8,128)(2,1)} %param.9) | copy-start | bytes 98308
  7.2 12.8 %copy-start.45 = (s32[2,4,128]{2,1,0:T(4,128)S(1)}, s32[2,4,128]{2,1,0:T(4,128)}, u32[]{:S(2)}) copy-start(s32[2,4,128]{2,1,0:T(4,128)} %param.7) | copy-start | bytes 12292
  7.2 13.4 %copy-start.44 = (bf16[27,256]{1,0:T(8,128)(2,1)S(1)}, bf16[27,256]{1,0:T(8,128)(2,1)}, u32[]{:S(2)}) copy-start(bf16[27,256]{1,0:T(8,128)(2,1)} %param.8) | copy-start | bytes 41476
  7.2 261.6 %all-gather.3.cloned.1.call-start = ((), (), s32[]{:S(2)}) async-start(), calls=%async_computation | async-start | bytes 33685504 | tf_op jit(solution)/shard_map/all_gather | solution.py:87
  8.6 18.4 %copy-start.6 = (bf16[2,4,128,256]{2,3,1,0:T(8,128)(2,1)}, bf16[2,4,128,256]{2,3,1,0:T(8,128)(2,1)S(1)}, u32[]{:S(2)}) copy-start(bf16[2,4,128,256]{2,3,1,0:T(8,128)(2,1)S(1)} %copy.86) | copy-start | bytes 1572868
  8.6 8.0 %collective-permute-start = (bf16[1,4,128,256]{2,3,1,0:T(8,128)(2,1)S(1)}, bf16[1,4,128,256]{2,3,1,0:T(8,128)(2,1)S(1)}, u32[]{:S(2)}, u32[]{:S(2)}) collective-permute-start(bf16[1,4,128,256]{2,3,1,0:T(8,128)(2,1)S(1)} %get-tuple-element.78), channel_id=1, source_target_pairs={{0,4},{4,8},{8,12},{12,16},{16,20},{20,24},{24,28},{28,32},{32,36}... | collective-permute-start | bytes 786440 | tf_op jit(solution)/shard_map/ppermute | solution.py:17
  8.7 7.9 %collective-permute-start.1 = (bf16[1,4,128,256]{2,3,1,0:T(8,128)(2,1)S(1)}, bf16[1,4,128,256]{2,3,1,0:T(8,128)(2,1)S(1)}, u32[]{:S(2)}, u32[]{:S(2)}) collective-permute-start(bf16[1,4,128,256]{2,3,1,0:T(8,128)(2,1)S(1)} %get-tuple-element.77), channel_id=1, source_target_pairs={{4,0},{8,4},{12,8},{16,12},{20,16},{24,20},{28,24},{32,28},{36,32}... | collective-permute-start | bytes 786440 | tf_op jit(solution)/shard_map/ppermute | solution.py:20
  14.1 18.2 %copy-start.46 = (f32[1,256]{1,0:T(1,128)}, f32[1,256]{1,0:T(1,128)S(1)}, u32[]{:S(2)}) copy-start(f32[1,256]{1,0:T(1,128)S(1)} %get-tuple-element.100) | copy-start | bytes 3076
  14.1 18.2 %copy-start.48 = (f32[1,256]{1,0:T(1,128)}, f32[1,256]{1,0:T(1,128)S(1)}, u32[]{:S(2)}) copy-start(f32[1,256]{1,0:T(1,128)S(1)} %get-tuple-element.101) | copy-start | bytes 3076
  14.2 18.2 %copy-start.50 = (f32[1,256]{1,0:T(1,128)}, f32[1,256]{1,0:T(1,128)S(1)}, u32[]{:S(2)}) copy-start(f32[1,256]{1,0:T(1,128)S(1)} %get-tuple-element.102) | copy-start | bytes 3076
  14.2 18.2 %copy-start.52 = (f32[1,256]{1,0:T(1,128)}, f32[1,256]{1,0:T(1,128)S(1)}, u32[]{:S(2)}) copy-start(f32[1,256]{1,0:T(1,128)S(1)} %get-tuple-element.103) | copy-start | bytes 3076
  14.2 18.2 %copy-start.54 = (f32[1,256]{1,0:T(1,128)}, f32[1,256]{1,0:T(1,128)S(1)}, u32[]{:S(2)}) copy-start(f32[1,256]{1,0:T(1,128)S(1)} %get-tuple-element.104) | copy-start | bytes 3076
  14.2 18.2 %copy-start.56 = (f32[1,256]{1,0:T(1,128)}, f32[1,256]{1,0:T(1,128)S(1)}, u32[]{:S(2)}) copy-start(f32[1,256]{1,0:T(1,128)S(1)} %get-tuple-element.105) | copy-start | bytes 3076
  16.6 15.8 %copy-start.12 = (bf16[1,4,128,256]{2,3,1,0:T(8,128)(2,1)}, bf16[1,4,128,256]{2,3,1,0:T(8,128)(2,1)S(1)}, u32[]{:S(2)}) copy-start(bf16[1,4,128,256]{2,3,1,0:T(8,128)(2,1)S(1)} %collective-permute-done) | copy-start | bytes 786436
  16.6 15.8 %copy-start.14 = (bf16[1,4,128,256]{2,3,1,0:T(8,128)(2,1)}, bf16[1,4,128,256]{2,3,1,0:T(8,128)(2,1)S(1)}, u32[]{:S(2)}) copy-start(bf16[1,4,128,256]{2,3,1,0:T(8,128)(2,1)S(1)} %collective-permute-done.1) | copy-start | bytes 786436
  16.7 9.3 %collective-permute-start.2 = (bf16[4,1,128,256]{2,3,1,0:T(8,128)(2,1)S(1)}, bf16[4,1,128,256]{2,3,1,0:T(8,128)(2,1)S(1)}, u32[]{:S(2)}, u32[]{:S(2)}) collective-permute-start(bf16[4,1,128,256]{2,3,1,0:T(8,128)(2,1)S(1)} %get-tuple-element.72), channel_id=1, source_target_pairs={{0,1},{1,2},{2,3},{3,0},{4,5},{5,6},{6,7},{7,4},{8,9},{9,10},{10,1... | collective-permute-start | bytes 786440 | tf_op jit(solution)/shard_map/ppermute | solution.py:17
  18.3 7.7 %collective-permute-start.3 = (bf16[4,1,128,256]{2,3,1,0:T(8,128)(2,1)S(1)}, bf16[4,1,128,256]{2,3,1,0:T(8,128)(2,1)S(1)}, u32[]{:S(2)}, u32[]{:S(2)}) collective-permute-start(bf16[4,1,128,256]{2,3,1,0:T(8,128)(2,1)S(1)} %get-tuple-element.73), channel_id=1, source_target_pairs={{1,0},{2,1},{3,2},{0,3},{5,4},{6,5},{7,6},{4,7},{9,8},{10,9},{11,1... | collective-permute-start | bytes 786440 | tf_op jit(solution)/shard_map/ppermute | solution.py:20
  20.6 11.8 %copy-start.58 = (f32[1,256]{1,0:T(1,128)}, f32[1,256]{1,0:T(1,128)S(1)}, u32[]{:S(2)}) copy-start(f32[1,256]{1,0:T(1,128)S(1)} %get-tuple-element.79) | copy-start | bytes 3076
  20.6 11.8 %copy-start.60 = (f32[1,256]{1,0:T(1,128)}, f32[1,256]{1,0:T(1,128)S(1)}, u32[]{:S(2)}) copy-start(f32[1,256]{1,0:T(1,128)S(1)} %get-tuple-element.80) | copy-start | bytes 3076
  20.6 11.8 %copy-start.62 = (f32[1,256]{1,0:T(1,128)}, f32[1,256]{1,0:T(1,128)S(1)}, u32[]{:S(2)}) copy-start(f32[1,256]{1,0:T(1,128)S(1)} %get-tuple-element.81) | copy-start | bytes 3076
  20.7 11.8 %copy-start.64 = (f32[1,256]{1,0:T(1,128)}, f32[1,256]{1,0:T(1,128)S(1)}, u32[]{:S(2)}) copy-start(f32[1,256]{1,0:T(1,128)S(1)} %get-tuple-element.82) | copy-start | bytes 3076
  20.7 11.8 %copy-start.66 = (f32[1,256]{1,0:T(1,128)}, f32[1,256]{1,0:T(1,128)S(1)}, u32[]{:S(2)}) copy-start(f32[1,256]{1,0:T(1,128)S(1)} %get-tuple-element.83) | copy-start | bytes 3076
  20.7 11.8 %copy-start.68 = (f32[1,256]{1,0:T(1,128)}, f32[1,256]{1,0:T(1,128)S(1)}, u32[]{:S(2)}) copy-start(f32[1,256]{1,0:T(1,128)S(1)} %get-tuple-element.84) | copy-start | bytes 3076
  20.7 11.8 %copy-start.70 = (f32[1,256]{1,0:T(1,128)}, f32[1,256]{1,0:T(1,128)S(1)}, u32[]{:S(2)}) copy-start(f32[1,256]{1,0:T(1,128)S(1)} %get-tuple-element.85) | copy-start | bytes 3076
  20.7 11.8 %copy-start.72 = (f32[1,256]{1,0:T(1,128)}, f32[1,256]{1,0:T(1,128)S(1)}, u32[]{:S(2)}) copy-start(f32[1,256]{1,0:T(1,128)S(1)} %get-tuple-element.86) | copy-start | bytes 3076
  20.7 11.8 %copy-start.74 = (f32[1,256]{1,0:T(1,128)}, f32[1,256]{1,0:T(1,128)S(1)}, u32[]{:S(2)}) copy-start(f32[1,256]{1,0:T(1,128)S(1)} %get-tuple-element.87) | copy-start | bytes 3076
  20.7 11.8 %copy-start.76 = (f32[1,256]{1,0:T(1,128)}, f32[1,256]{1,0:T(1,128)S(1)}, u32[]{:S(2)}) copy-start(f32[1,256]{1,0:T(1,128)S(1)} %get-tuple-element.88) | copy-start | bytes 3076
  20.7 11.8 %copy-start.78 = (f32[1,256]{1,0:T(1,128)}, f32[1,256]{1,0:T(1,128)S(1)}, u32[]{:S(2)}) copy-start(f32[1,256]{1,0:T(1,128)S(1)} %get-tuple-element.89) | copy-start | bytes 3076
  20.7 11.8 %copy-start.80 = (f32[1,256]{1,0:T(1,128)}, f32[1,256]{1,0:T(1,128)S(1)}, u32[]{:S(2)}) copy-start(f32[1,256]{1,0:T(1,128)S(1)} %get-tuple-element.90) | copy-start | bytes 3076
  20.7 11.8 %copy-start.82 = (f32[1,256]{1,0:T(1,128)}, f32[1,256]{1,0:T(1,128)S(1)}, u32[]{:S(2)}) copy-start(f32[1,256]{1,0:T(1,128)S(1)} %get-tuple-element.91) | copy-start | bytes 3076
  20.8 11.8 %copy-start.84 = (f32[1,256]{1,0:T(1,128)}, f32[1,256]{1,0:T(1,128)S(1)}, u32[]{:S(2)}) copy-start(f32[1,256]{1,0:T(1,128)S(1)} %get-tuple-element.92) | copy-start | bytes 3076
  20.8 11.8 %copy-start.86 = (f32[1,256]{1,0:T(1,128)}, f32[1,256]{1,0:T(1,128)S(1)}, u32[]{:S(2)}) copy-start(f32[1,256]{1,0:T(1,128)S(1)} %get-tuple-element.93) | copy-start | bytes 3076
  20.8 11.8 %copy-start.88 = (f32[1,256]{1,0:T(1,128)}, f32[1,256]{1,0:T(1,128)S(1)}, u32[]{:S(2)}) copy-start(f32[1,256]{1,0:T(1,128)S(1)} %get-tuple-element.94) | copy-start | bytes 3076
  20.8 11.8 %copy-start.90 = (f32[1,256]{1,0:T(1,128)}, f32[1,256]{1,0:T(1,128)S(1)}, u32[]{:S(2)}) copy-start(f32[1,256]{1,0:T(1,128)S(1)} %get-tuple-element.95) | copy-start | bytes 3076
  20.8 11.8 %copy-start.92 = (f32[1,256]{1,0:T(1,128)}, f32[1,256]{1,0:T(1,128)S(1)}, u32[]{:S(2)}) copy-start(f32[1,256]{1,0:T(1,128)S(1)} %get-tuple-element.96) | copy-start | bytes 3076
  20.8 11.8 %copy-start.94 = (f32[1,256]{1,0:T(1,128)}, f32[1,256]{1,0:T(1,128)S(1)}, u32[]{:S(2)}) copy-start(f32[1,256]{1,0:T(1,128)S(1)} %get-tuple-element.97) | copy-start | bytes 3076
  32.7 89.4 %copy-start.107 = (f32[256]{0:T(256)S(1)}, f32[256]{0:T(256)}, u32[]{:S(2)}) copy-start(f32[256]{0:T(256)} %param.10) | copy-start | bytes 3076
  121.3 422.9 %all-reduce.4.cloned.1.call-start = ((), (), s32[]{:S(2)}) async-start(), calls=%async_computation.1 | async-start | bytes 524288 | tf_op jit(solution)/shard_map/psum | solution.py:109
  295.2 249.1 %copy-start.106 = (f32[4]{0:T(128)S(1)}, f32[4]{0:T(128)}, u32[]{:S(2)}) copy-start(f32[4]{0:T(128)} %copy-done.105) | copy-start | bytes 52
  544.3 15.1 %copy-start.37 = (f32[4,64,64]{2,1,0:T(8,128)S(1)}, f32[4,64,64]{2,1,0:T(8,128)}, u32[]{:S(2)}) copy-start(f32[4,64,64]{2,1,0:T(8,128)} %copy-done.36) | copy-start | bytes 196612
  545.7 14.5 %copy-start.29 = (f32[4,64,64]{2,1,0:T(8,128)S(1)}, f32[4,64,64]{2,1,0:T(8,128)}, u32[]{:S(2)}) copy-start(f32[4,64,64]{2,1,0:T(8,128)} %copy-done.28) | copy-start | bytes 196612
  548.4 12.6 %copy-start.21 = (f32[4,64,64]{2,1,0:T(8,128)S(1)}, f32[4,64,64]{2,1,0:T(8,128)}, u32[]{:S(2)}) copy-start(f32[4,64,64]{2,1,0:T(8,128)} %copy-done.20) | copy-start | bytes 196612
  565.7 14.0 %copy-start.13 = (bf16[1,4,128,256]{2,3,1,0:T(8,128)(2,1)S(1)}, bf16[1,4,128,256]{2,3,1,0:T(8,128)(2,1)}, u32[]{:S(2)}) copy-start(bf16[1,4,128,256]{2,3,1,0:T(8,128)(2,1)} %copy-done.12) | copy-start | bytes 786436
  575.7 88.9 %collective-permute-start.4 = (bf16[1,4,128,256]{2,3,1,0:T(8,128)(2,1)}, bf16[1,4,128,256]{2,3,1,0:T(8,128)(2,1)}, u32[]{:S(2)}, u32[]{:S(2)}) collective-permute-start(bf16[1,4,128,256]{2,3,1,0:T(8,128)(2,1)} %get-tuple-element.75), channel_id=1, source_target_pairs={{0,4},{4,8},{8,12},{12,16},{16,20},{20,24},{24,28},{28,32},{32,36}... | collective-permute-start | bytes 786440 | tf_op jit(solution)/shard_map/ppermute | solution.py:17
  576.4 88.2 %collective-permute-start.5 = (bf16[1,4,128,256]{2,3,1,0:T(8,128)(2,1)}, bf16[1,4,128,256]{2,3,1,0:T(8,128)(2,1)}, u32[]{:S(2)}, u32[]{:S(2)}) collective-permute-start(bf16[1,4,128,256]{2,3,1,0:T(8,128)(2,1)} %get-tuple-element.76), channel_id=1, source_target_pairs={{4,0},{8,4},{12,8},{16,12},{20,16},{24,20},{28,24},{32,28},{36,32}... | collective-permute-start | bytes 786440 | tf_op jit(solution)/shard_map/ppermute | solution.py:20
  586.3 88.2 %copy-start.5 = (bf16[2,4,128,4,64]{2,4,3,1,0:T(8,128)(2,1)S(1)}, bf16[2,4,128,4,64]{2,4,3,1,0:T(8,128)(2,1)}, u32[]{:S(2)}) copy-start(bf16[2,4,128,4,64]{2,4,3,1,0:T(8,128)(2,1)} %copy-done.4) | copy-start | bytes 1572868
  665.7 8.8 %collective-permute-start.6 = (bf16[4,1,128,256]{2,3,1,0:T(8,128)(2,1)S(1)}, bf16[4,1,128,256]{2,3,1,0:T(8,128)(2,1)S(1)}, u32[]{:S(2)}, u32[]{:S(2)}) collective-permute-start(bf16[4,1,128,256]{2,3,1,0:T(8,128)(2,1)S(1)} %get-tuple-element.68), channel_id=1, source_target_pairs={{0,1},{1,2},{2,3},{3,0},{4,5},{5,6},{6,7},{7,4},{8,9},{9,10},{10,1... | collective-permute-start | bytes 786440 | tf_op jit(solution)/shard_map/ppermute | solution.py:17
  665.8 8.7 %collective-permute-start.7 = (bf16[4,1,128,256]{2,3,1,0:T(8,128)(2,1)S(1)}, bf16[4,1,128,256]{2,3,1,0:T(8,128)(2,1)S(1)}, u32[]{:S(2)}, u32[]{:S(2)}) collective-permute-start(bf16[4,1,128,256]{2,3,1,0:T(8,128)(2,1)S(1)} %get-tuple-element.69), channel_id=1, source_target_pairs={{1,0},{2,1},{3,2},{0,3},{5,4},{6,5},{7,6},{4,7},{9,8},{10,9},{11,1... | collective-permute-start | bytes 786440 | tf_op jit(solution)/shard_map/ppermute | solution.py:20
  (71 other events, 387.4 us)
Sparse Core Ops, SparseCore 0:
  121.5 147.2 all-gather.2
  296.3 247.9 all-reduce.3
